TPU v7x, 1024 devices: a whole 8x8x8 slice. The times are simulated.
1024 devices in a mesh: pipe: 16 (over x_hi, y), expert: 8 (over x_lo, core), dp: 8 (over z).
Axes of the slice: x: 8 (x_hi: 2, x_lo: 4; x = x_hi * 4 + x_lo), y: 8, z: 8, core: 2. Of those that a mesh axis runs over, the one named last changes fastest.
Arguments:
- tokens: bfloat16 [1536, 6144], P('expert', 'dp'), may hold values from -6 to 6
- expert_ids: int32 [1536, 2], P('expert'), may hold values from 0 to 7, all different within a row; in each aligned block of 192 rows (0 to 191, 192 to 383, ...) at most 60 rows name the same one
- gate_share: float32 [1536, 2], P('expert'), may hold values from 0.1 to 1
- gate_proj: bfloat16 [8, 6144, 8192], P('expert', 'dp', 'pipe'), may hold values from -0.078125 to 0.078125
- up_proj: bfloat16 [8, 6144, 8192], P('expert', 'dp', 'pipe'), may hold values from -0.078125 to 0.078125
- down_proj: bfloat16 [8, 8192, 6144], P('expert', 'pipe', 'dp'), may hold values from -0.0625 to 0.0625
Outputs:
- layer_out: bfloat16 [1536, 6144], P('expert', 'dp')
Inputs may be any that keep to these rules, and one draw needn't show every extreme that they name: `expert_ids`: each token names two different experts. Among the 192 tokens of one source block, no expert is named by more than 60 of them, and in every draw some expert is named by exactly 60 in some block.
All inputs are finite; a program needn't handle non-finite values.
Results may differ from a plain program's by a relative error of at most 0.0049.
Values may be sent and summed in bfloat16 or wider, within the bound.
No kernel may reach another device: no remote copies, remote signals or barrier semaphores. Data moves between devices by JAX's collectives and lax.ppermute only.
A program may use at most 32 MiB of HBM per device.

v0:
```python
import jax
import jax.numpy as jnp
from jax import lax
from jax.sharding import PartitionSpec as P


def swiglu(gate_up):
    middle = gate_up.shape[1] // 2
    return (jax.nn.silu(gate_up[:, :middle]) * gate_up[:, middle:]).astype(jnp.bfloat16)


def body(tokens, expert_ids, gate_share, gate_proj, up_proj, down_proj):
    tok_rows = tokens.shape[0]
    columns = tokens.shape[1]
    groups = lax.axis_size("expert")
    capacity = min(tok_rows, 5 * tok_rows // (2 * groups))
    slots_all = groups * capacity
    share = columns // lax.axis_size("pipe")
    choices_flat = expert_ids.reshape(-1)
    onehot = (choices_flat[:, None] == jnp.arange(groups, dtype=jnp.int32)[None, :]).astype(
        jnp.int32
    )
    before = jnp.cumsum(onehot, axis=0) - onehot
    slot_rank = jnp.sum(before * onehot, axis=1)
    target = choices_flat * capacity + slot_rank
    placed = (target[:, None] == jnp.arange(slots_all, dtype=jnp.int32)[None, :]).reshape(
        tok_rows, 2, slots_all
    )
    dispatch_map = jnp.sum(placed.astype(jnp.bfloat16), axis=1)
    weighting = jnp.sum(placed.astype(jnp.float32) * gate_share[:, :, None], axis=1)
    outbound = lax.dot_general(
        dispatch_map, tokens, (((0,), (0,)), ((), ())), preferred_element_type=jnp.float32
    )
    outbound = outbound.astype(jnp.bfloat16).reshape(groups, capacity, columns)
    received = lax.all_to_all(outbound, "expert", split_axis=0, concat_axis=0, tiled=True).reshape(
        slots_all, columns
    )
    gate_part = jnp.dot(received, gate_proj[0], preferred_element_type=jnp.float32)
    up_part = jnp.dot(received, up_proj[0], preferred_element_type=jnp.float32)
    gate_up = jnp.concatenate([gate_part, up_part], axis=1)
    summed = lax.psum(gate_up, "dp")
    hidden = swiglu(summed)
    down_local = down_proj[0]
    feature_share = lax.psum_scatter(
        lax.dot_general(
            down_local, hidden, (((0,), (1,)), ((), ())), preferred_element_type=jnp.float32
        ),
        "pipe",
        scatter_dimension=0,
        tiled=True,
    )
    returned = lax.all_to_all(
        feature_share.reshape(share, groups, capacity),
        "expert",
        split_axis=1,
        concat_axis=1,
        tiled=True,
    )
    returned = returned.reshape(share, slots_all)
    result = lax.dot_general(
        weighting,
        returned,
        (((1,), (1,)), ((), ())),
        precision=lax.Precision.HIGHEST,
        preferred_element_type=jnp.float32,
    )
    rounded = result.astype(jnp.bfloat16)
    return lax.all_gather(rounded, "pipe", axis=1, tiled=True)


def solution(mesh):
    return jax.shard_map(
        body,
        mesh=mesh,
        in_specs=(
            P("expert", "dp"),
            P("expert", None),
            P("expert", None),
            P("expert", "dp", "pipe"),
            P("expert", "dp", "pipe"),
            P("expert", "pipe", "dp"),
        ),
        out_specs=P("expert", "dp"),
        check_vma=False,
    )
```

profile of v0, /device:TPU:10, one launch (start us, length us, event | category | flops | bytes accessed | tf_op | source)
XLA Modules:
  0.0 450.7 jit_solution(14769084762784224416)
XLA Ops:
  6.5 0.9 copy.35
  7.4 0.1 eq.43
  7.6 0.1 eq.39
  7.7 0.9 reduce-window.6
  8.6 0.2 slice_reduce_fusion
  8.9 0.1 reduce_sum.33
  9.2 0.7 multiply_add_fusion
  9.9 0.1 fusion.9
  10.0 1.4 convolution_convert_fusion
  11.4 0.1 reshape.49
  11.5 22.6 %all_to_all.10 = bf16[8,60,768]{2,1,0:T(8,128)(2,1)S(1)} all-to-all(bf16[8,60,768]{2,1,0:T(8,128)(2,1)S(1)} %reshape.49), channel_id=1, replica_groups=mesh['pipe'=16,'expert'=8,'dp'=8] {'expert'}, dimensions={0} | all-to-all | bytes 1474560 | tf_op jit(solution)/shard_map/all_to_all | solution.py:35
  34.2 0.1 reshape.50
  34.3 0.5 fusion.2
  34.9 0.6 copy-done.2
  35.5 0.5 fusion.4
  36.0 1.4 pad_maximum_fusion
  37.5 106.5 %all-reduce.2.cloned.1.call-done = f32[480,1024]{1,0:T(8,128)} async-done(((f32[480,1024]{1,0:T(8,128)}), f32[480,1024]{1,0:T(8,128)}) %all-reduce.2.cloned.1.call-update) | async-done | bytes 1966096 | tf_op jit(solution)/shard_map/psum | solution.py:41
  144.0 2.2 convolution_bitcast_fusion
  146.2 1.6 copy.44
  147.8 227.9 %reduce-scatter.4.cloned.1.call-done = f32[48,480]{1,0:T(8,128)} async-done(((f32[768,480]{1,0:T(8,128)}), f32[48,480]{1,0:T(8,128)}) %reduce-scatter.4.cloned.1.call-update) | async-done | bytes 92176
  375.7 1.0 reshape.56
  376.8 0.9 reshape.58
  377.6 5.5 %all-to-all-start.1 = ((f32[8,1,2880]{2,1,0:T(1,128)}), f32[8,1,2880]{2,1,0:T(1,128)S(1)}, u32[]{:S(2)}, u32[]{:S(2)}) async-start(f32[8,1,2880]{2,1,0:T(1,128)} %reshape.58), calls=%async_computation.1 | async-start | bytes 188416 | tf_op jit(solution)/shard_map/all_to_all | solution.py:52
  383.2 0.2 select_reduce_fusion
  383.3 4.9 %all-to-all-done.1 = f32[8,1,2880]{2,1,0:T(1,128)S(1)} async-done(((f32[8,1,2880]{2,1,0:T(1,128)}), f32[8,1,2880]{2,1,0:T(1,128)S(1)}, u32[]{:S(2)}, u32[]{:S(2)}) %all-to-all-start.1) | async-done | bytes 92192 | tf_op jit(solution)/shard_map/all_to_all | solution.py:52
  388.2 0.5 broadcast.36
  388.7 0.9 reduce.3
  389.6 0.1 reshape.59
  389.8 0.1 reshape.52
  390.0 0.5 convolution_convert_fusion.1
  390.5 52.5 %all_gather.3 = bf16[192,768]{0,1:T(8,128)(2,1)S(1)} all-gather(bf16[192,48]{0,1:T(8,128)(2,1)S(1)} %convolution_convert_fusion.1), channel_id=1, replica_groups=mesh['pipe'=16,'expert'=8,'dp'=8] {'pipe'}, dimensions={1}, use_global_device_ids=true | all-gather | bytes 313344 | tf_op jit(solution)/shard_map/all_gather | solution.py:68
  443.0 0.9 copy.41
  (17 shorter events, 0.4 us)
Async XLA Ops:
  6.5 137.5 %copy-start = (bf16[1,512,768]{2,1,0:T(8,128)(2,1)S(1)}, bf16[1,512,768]{2,1,0:T(8,128)(2,1)}, u32[]{:S(2)}) copy-start(bf16[1,512,768]{2,1,0:T(8,128)(2,1)} %param.11) | copy-start | bytes 2359300
  6.5 137.5 %all-reduce.2.cloned.1.call-start = ((), (), s32[]{:S(2)}) async-start(), calls=%async_computation.3 | async-start | bytes 3932160 | tf_op jit(solution)/shard_map/psum | solution.py:41
  11.4 22.9 %copy-start.1 = (bf16[1,768,512]{2,1,0:T(8,128)(2,1)S(1)}, bf16[1,768,512]{2,1,0:T(8,128)(2,1)}, u32[]{:S(2)}) copy-start(bf16[1,768,512]{2,1,0:T(8,128)(2,1)} %param.10) | copy-start | bytes 2359300
  34.3 1.1 copy-start.2
  37.4 338.3 %reduce-scatter.4.cloned.1.call-start = ((), (), s32[]{:S(2)}) async-start(), calls=%async_computation.4 | async-start | bytes 1671168
  147.8 235.3 %copy-start.3 = (f32[192,2]{0,1:T(2,128)S(1)}, f32[192,2]{0,1:T(2,128)}, u32[]{:S(2)}) copy-start(f32[192,2]{0,1:T(2,128)} %param.8) | copy-start | bytes 4612
  377.6 10.6 %all-to-all-start.1 = ((f32[8,1,2880]{2,1,0:T(1,128)}), f32[8,1,2880]{2,1,0:T(1,128)S(1)}, u32[]{:S(2)}, u32[]{:S(2)}) async-start(f32[8,1,2880]{2,1,0:T(1,128)} %reshape.58), calls=%async_computation.1 | async-start | bytes 188416 | tf_op jit(solution)/shard_map/all_to_all | solution.py:52
Sparse Core Ops, SparseCore 0:
  37.6 106.4 all-reduce.1
  149.6 226.0 reduce-scatter.3
where the time goes:
time: 451 us
  waiting for transfers between devices  339 us (75%)
  blocking collectives  75.2 us (17%)
  between operations  13.6 us (3%)
  local copies, waits for them, and re-layouts  7.7 us (2%)
  starting transfers between devices  5.55 us (1%)
  matrix products  5.11 us (1%)
    unnamed x3, waiting for transfers between devices  228 us
    psum x1, waiting for transfers between devices, body(): summed = lax.psum(gate_up, 'dp')  107 us
    all_gather x1, blocking collectives, body(): return lax.all_gather(rounded, 'pipe', axis=1, tiled=True)  52.5 us
    all_to_all x1, blocking collectives, body(): lax.all_to_all(outbound, 'expert', split_axis=0, concat_axis=0, tiled=True)  22.6 us
  transfers between devices with their start and end apart: 3, of which 3 were waited for; matrix products, arithmetic and copies ran while one was open for 0% of the time, Pallas kernels for 0%

commit v1 on v0

--- a/solution.py
+++ b/solution.py
@@ -9,13 +9,20 @@
     return (jax.nn.silu(gate_up[:, :middle]) * gate_up[:, middle:]).astype(jnp.bfloat16)
 
 
+def gather_rows(part, axis):
+    count = lax.axis_size(axis)
+    copies = jnp.broadcast_to(part[None], (count,) + part.shape)
+    gathered = lax.all_to_all(copies, axis, split_axis=0, concat_axis=0, tiled=True)
+    return gathered.reshape((count * part.shape[0],) + part.shape[1:])
+
+
 def body(tokens, expert_ids, gate_share, gate_proj, up_proj, down_proj):
     tok_rows = tokens.shape[0]
     columns = tokens.shape[1]
     groups = lax.axis_size("expert")
+    n_pipe = lax.axis_size("pipe")
     capacity = min(tok_rows, 5 * tok_rows // (2 * groups))
     slots_all = groups * capacity
-    share = columns // lax.axis_size("pipe")
     choices_flat = expert_ids.reshape(-1)
     onehot = (choices_flat[:, None] == jnp.arange(groups, dtype=jnp.int32)[None, :]).astype(
         jnp.int32
@@ -38,34 +45,40 @@
     gate_part = jnp.dot(received, gate_proj[0], preferred_element_type=jnp.float32)
     up_part = jnp.dot(received, up_proj[0], preferred_element_type=jnp.float32)
     gate_up = jnp.concatenate([gate_part, up_part], axis=1)
-    summed = lax.psum(gate_up, "dp")
-    hidden = swiglu(summed)
-    down_local = down_proj[0]
-    feature_share = lax.psum_scatter(
-        lax.dot_general(
-            down_local, hidden, (((0,), (1,)), ((), ())), preferred_element_type=jnp.float32
+    n_dp = lax.axis_size("dp")
+    summed = jnp.sum(
+        lax.all_to_all(
+            gate_up.reshape(n_dp, slots_all // n_dp, -1), "dp", split_axis=0, concat_axis=0, tiled=True
         ),
-        "pipe",
-        scatter_dimension=0,
+        axis=0,
+    )
+    hidden = gather_rows(swiglu(summed), "dp")
+    expert_part = jnp.dot(hidden, down_proj[0], preferred_element_type=jnp.float32)
+    returned = lax.all_to_all(
+        expert_part.reshape(groups, capacity, columns),
+        "expert",
+        split_axis=0,
+        concat_axis=0,
         tiled=True,
-    )
-    returned = lax.all_to_all(
-        feature_share.reshape(share, groups, capacity),
-        "expert",
-        split_axis=1,
-        concat_axis=1,
-        tiled=True,
-    )
-    returned = returned.reshape(share, slots_all)
-    result = lax.dot_general(
+    ).reshape(slots_all, columns)
+    combined = lax.dot_general(
         weighting,
         returned,
-        (((1,), (1,)), ((), ())),
+        (((1,), (0,)), ((), ())),
         precision=lax.Precision.HIGHEST,
         preferred_element_type=jnp.float32,
     )
-    rounded = result.astype(jnp.bfloat16)
-    return lax.all_gather(rounded, "pipe", axis=1, tiled=True)
+    share = jnp.sum(
+        lax.all_to_all(
+            combined.reshape(n_pipe, tok_rows // n_pipe, columns),
+            "pipe",
+            split_axis=0,
+            concat_axis=0,
+            tiled=True,
+        ),
+        axis=0,
+    )
+    return gather_rows(share.astype(jnp.bfloat16), "pipe")
 
 
 def solution(mesh):

time: 451 us -> 224 us (0.50)
  the two profiles are of different devices: /device:TPU:10 before, /device:TPU:2 now
where the time goes in v1:
time: 224 us
  blocking collectives  168 us (75%)
  waiting for transfers between devices  34.1 us (15%)
  matrix products  7.05 us (3%)
  local copies, waits for them, and re-layouts  6.17 us (3%)
  starting transfers between devices  6.02 us (3%)
  other arithmetic  2.4 us (1%)
    all_to_all x1, blocking collectives, body(): lax.all_to_all(gate_up.reshape(n_dp, slots_all // n_dp, -1), 'dp', split_...  56.8 us
    all_to_all x2, blocking collectives, gather_rows(): lax.all_to_all(copies, axis, split_axis=0, concat_axis=0, tiled=True)  42.5 us
    all_to_all x1, blocking collectives, body(): lax.all_to_all(outbound, 'expert', split_axis=0, concat_axis=0, tiled=True)  34.4 us
    all_to_all x1, waiting for transfers between devices, body(): lax.all_to_all(expert_part.reshape(groups, capacity, columns), 'expert',...  34.1 us
    all_to_all x1, blocking collectives, body(): lax.all_to_all(combined.reshape(n_pipe, tok_rows // n_pipe, columns), 'pi...  34 us
    all_to_all x1, starting transfers between devices, body(): lax.all_to_all(expert_part.reshape(groups, capacity, columns), 'expert',...  6.02 us
  transfers between devices with their start and end apart: 1, of which 1 were waited for; matrix products, arithmetic and copies ran while one was open for 0% of the time, Pallas kernels for 0%

profile of v1, /device:TPU:2, one launch (start us, length us, event | category | flops | bytes accessed | tf_op | source)
XLA Modules:
  0.0 223.6 jit_solution(2926891444533245218)
XLA Ops:
  0.0 0.9 copy.29
  0.9 0.1 eq.43
  1.0 0.1 eq.39
  1.2 0.9 reduce-window.6
  2.0 0.2 slice_reduce_fusion
  2.3 0.1 fusion.10
  2.4 0.1 reduce_sum.51
  2.5 0.1 copy.31
  2.6 0.7 multiply_add_fusion
  3.3 0.1 fusion.7
  3.5 1.4 convolution_convert_fusion
  4.9 0.1 reshape.62
  5.0 34.4 %all_to_all.30 = bf16[8,60,768]{2,1,0:T(8,128)(2,1)S(1)} all-to-all(bf16[8,60,768]{2,1,0:T(8,128)(2,1)S(1)} %reshape.62), channel_id=1, replica_groups=mesh['pipe'=16,'expert'=8,'dp'=8] {'expert'}, dimensions={0} | all-to-all | bytes 1474560 | tf_op jit(solution)/shard_map/all_to_all | solution.py:42
  39.4 0.1 reshape.63
  39.5 0.5 fusion.2
  40.1 0.6 copy-done.2
  40.6 0.5 fusion.4
  41.2 0.1 pad_maximum_fusion
  41.3 1.5 reshape.64
  42.9 56.8 %all_to_all.31 = f32[8,60,1024]{2,1,0:T(8,128)S(1)} all-to-all(f32[8,60,1024]{2,1,0:T(8,128)} %reshape.64), channel_id=1, replica_groups=mesh['pipe'=16,'expert'=8,'dp'=8] {'dp'}, dimensions={0} | all-to-all | bytes 3932160 | tf_op jit(solution)/shard_map/all_to_all | solution.py:50
  99.7 0.1 reduce_sum.54
  100.0 18.5 %all_to_all.32 = bf16[8,60,512]{2,1,0:T(8,128)(2,1)S(1)} all-to-all(bf16[8,60,512]{2,1,0:T(8,128)(2,1)S(1)} %broadcast_in_dim.4), channel_id=1, replica_groups=mesh['pipe'=16,'expert'=8,'dp'=8] {'dp'}, dimensions={0} | all-to-all | bytes 983040 | tf_op jit(solution)/shard_map/all_to_all | solution.py:15
  118.4 1.7 fusion
  120.2 6.0 %all-to-all-start.3 = ((f32[8,60,768]{2,1,0:T(8,128)}), f32[8,60,768]{2,1,0:T(8,128)S(1)}, u32[]{:S(2)}, u32[]{:S(2)}) async-start(f32[8,60,768]{2,1,0:T(8,128)} %fusion), calls=%async_computation.3 | async-start | bytes 3145728 | tf_op jit(solution)/shard_map/all_to_all | solution.py:57
  126.2 0.2 select_reduce_fusion
  126.4 34.1 %all-to-all-done.3 = f32[8,60,768]{2,1,0:T(8,128)S(1)} async-done(((f32[8,60,768]{2,1,0:T(8,128)}), f32[8,60,768]{2,1,0:T(8,128)S(1)}, u32[]{:S(2)}, u32[]{:S(2)}) %all-to-all-start.3) | async-done | bytes 1474592 | tf_op jit(solution)/shard_map/all_to_all | solution.py:57
  160.5 1.3 reshape.68
  161.8 2.9 %fusion.12 = f32[16,12,768]{2,1,0:T(8,128)S(1)} fusion(f32[16,12,480]{2,1,0:T(8,128)S(1)} %dot_general.17, f32[480,768,1]{1,0,2:T(8,128)} %reshape.68), kind=kOutput, calls=%fused_computation.22 | convolution fusion | flops 849346560 | bytes 2433024 | tf_op jit(solution)/shard_map/dot_general | solution.py:64
  164.7 34.0 %all_to_all.33 = f32[16,12,768]{2,1,0:T(8,128)S(1)} all-to-all(f32[16,12,768]{2,1,0:T(8,128)S(1)} %fusion.12), channel_id=1, replica_groups=mesh['pipe'=16,'expert'=8,'dp'=8] {'pipe'}, dimensions={0} | all-to-all | bytes 1179648 | tf_op jit(solution)/shard_map/all_to_all | solution.py:72
  198.7 0.1 reduce_sum.55
  198.8 24.0 %all_to_all.34 = bf16[16,12,768]{2,1,0:T(8,128)(2,1)S(1)} all-to-all(bf16[16,12,768]{2,1,0:T(8,128)(2,1)S(1)} %broadcast_in_dim.5), channel_id=1, replica_groups=mesh['pipe'=16,'expert'=8,'dp'=8] {'pipe'}, dimensions={0} | all-to-all | bytes 589824 | tf_op jit(solution)/shard_map/all_to_all | solution.py:15
  222.8 0.8 reshape.66
  (13 shorter events, 0.2 us)
Async XLA Ops:
  0.0 118.4 %copy-start = (bf16[1,512,768]{2,1,0:T(8,128)(2,1)S(1)}, bf16[1,512,768]{2,1,0:T(8,128)(2,1)}, u32[]{:S(2)}) copy-start(bf16[1,512,768]{2,1,0:T(8,128)(2,1)} %param.11) | copy-start | bytes 2359300
  5.0 34.5 %copy-start.1 = (bf16[1,768,512]{2,1,0:T(8,128)(2,1)S(1)}, bf16[1,768,512]{2,1,0:T(8,128)(2,1)}, u32[]{:S(2)}) copy-start(bf16[1,768,512]{2,1,0:T(8,128)(2,1)} %param.10) | copy-start | bytes 2359300
  39.5 1.1 copy-start.2
  120.2 6.0 %copy-start.3 = (f32[192,2]{0,1:T(2,128)S(1)}, f32[192,2]{0,1:T(2,128)}, u32[]{:S(2)}) copy-start(f32[192,2]{0,1:T(2,128)} %param.8) | copy-start | bytes 4612
  120.2 40.4 %all-to-all-start.3 = ((f32[8,60,768]{2,1,0:T(8,128)}), f32[8,60,768]{2,1,0:T(8,128)S(1)}, u32[]{:S(2)}, u32[]{:S(2)}) async-start(f32[8,60,768]{2,1,0:T(8,128)} %fusion), calls=%async_computation.3 | async-start | bytes 3145728 | tf_op jit(solution)/shard_map/all_to_all | solution.py:57

commit v2 on v1

--- a/solution.py
+++ b/solution.py
@@ -55,7 +55,7 @@
     hidden = gather_rows(swiglu(summed), "dp")
     expert_part = jnp.dot(hidden, down_proj[0], preferred_element_type=jnp.float32)
     returned = lax.all_to_all(
-        expert_part.reshape(groups, capacity, columns),
+        expert_part.astype(jnp.bfloat16).reshape(groups, capacity, columns),
         "expert",
         split_axis=0,
         concat_axis=0,
@@ -63,7 +63,7 @@
     ).reshape(slots_all, columns)
     combined = lax.dot_general(
         weighting,
-        returned,
+        returned.astype(jnp.float32),
         (((1,), (0,)), ((), ())),
         precision=lax.Precision.HIGHEST,
         preferred_element_type=jnp.float32,

time: 224 us -> 204 us (0.911)
  waiting for transfers between devices: 34.1 us -> 17.3 us
  matrix products: 7.05 us -> 3.81 us
    all_to_all x1, waiting for transfers between devices: 34.1 us -> 17.3 us  [body(): lax.all_to_all(expert_part.astype(jnp.bfloat16).reshape(groups, capacity,...]
where the time goes in v2:
time: 204 us; the launch traced here: 203 us
  blocking collectives  168 us (82%)
  waiting for transfers between devices  17.3 us (8%)
  local copies, waits for them, and re-layouts  6.13 us (3%)
  starting transfers between devices  5.88 us (3%)
  matrix products  3.81 us (2%)
  other arithmetic  2.4 us (1%)
    all_to_all x1, blocking collectives, body(): lax.all_to_all(gate_up.reshape(n_dp, slots_all // n_dp, -1), 'dp', split_...  56.8 us
    all_to_all x2, blocking collectives, gather_rows(): lax.all_to_all(copies, axis, split_axis=0, concat_axis=0, tiled=True)  42.5 us
    all_to_all x1, blocking collectives, body(): lax.all_to_all(outbound, 'expert', split_axis=0, concat_axis=0, tiled=True)  34.4 us
    all_to_all x1, blocking collectives, body(): lax.all_to_all(combined.reshape(n_pipe, tok_rows // n_pipe, columns), 'pi...  34 us
    all_to_all x1, waiting for transfers between devices, body(): lax.all_to_all(expert_part.astype(jnp.bfloat16).reshape(groups, capacity,...  17.3 us
    all_to_all x1, starting transfers between devices, body(): lax.all_to_all(expert_part.astype(jnp.bfloat16).reshape(groups, capacity,...  5.88 us
  transfers between devices with their start and end apart: 1, of which 1 were waited for; matrix products, arithmetic and copies ran while one was open for 0% of the time, Pallas kernels for 0%

profile of v2, /device:TPU:2, one launch (start us, length us, event | category | flops | bytes accessed | tf_op | source)
XLA Modules:
  0.0 203.3 jit_solution(14200553573403016136)
XLA Ops:
  0.0 0.9 copy.29
  0.9 0.1 eq.43
  1.0 0.1 eq.39
  1.2 0.9 reduce-window.6
  2.0 0.2 slice_reduce_fusion
  2.3 0.1 fusion.9
  2.4 0.1 reduce_sum.51
  2.6 0.7 multiply_add_fusion
  3.3 0.1 fusion.6
  3.5 1.4 convolution_convert_fusion.1
  4.9 0.1 reshape.64
  5.0 34.4 %all_to_all.30 = bf16[8,60,768]{2,1,0:T(8,128)(2,1)S(1)} all-to-all(bf16[8,60,768]{2,1,0:T(8,128)(2,1)S(1)} %reshape.64), channel_id=1, replica_groups=mesh['pipe'=16,'expert'=8,'dp'=8] {'expert'}, dimensions={0} | all-to-all | bytes 1474560 | tf_op jit(solution)/shard_map/all_to_all | solution.py:42
  39.4 0.1 reshape.65
  39.5 0.5 fusion.1
  40.1 0.6 copy-done.2
  40.6 0.5 fusion.3
  41.2 0.1 pad_maximum_fusion
  41.3 1.5 reshape.66
  42.9 56.8 %all_to_all.31 = f32[8,60,1024]{2,1,0:T(8,128)S(1)} all-to-all(f32[8,60,1024]{2,1,0:T(8,128)} %reshape.66), channel_id=1, replica_groups=mesh['pipe'=16,'expert'=8,'dp'=8] {'dp'}, dimensions={0} | all-to-all | bytes 3932160 | tf_op jit(solution)/shard_map/all_to_all | solution.py:50
  99.7 0.1 reduce_sum.54
  100.0 18.5 %all_to_all.32 = bf16[8,60,512]{2,1,0:T(8,128)(2,1)S(1)} all-to-all(bf16[8,60,512]{2,1,0:T(8,128)(2,1)S(1)} %broadcast_in_dim.4), channel_id=1, replica_groups=mesh['pipe'=16,'expert'=8,'dp'=8] {'dp'}, dimensions={0} | all-to-all | bytes 983040 | tf_op jit(solution)/shard_map/all_to_all | solution.py:15
  118.4 0.1 reshape.67
  118.5 0.5 convolution_convert_fusion
  119.1 1.0 reshape.68
  120.1 5.9 %all-to-all-start.3 = ((bf16[8,60,768]{2,1,0:T(8,128)(2,1)}), bf16[8,60,768]{2,1,0:T(8,128)(2,1)S(1)}, u32[]{:S(2)}, u32[]{:S(2)}) async-start(bf16[8,60,768]{2,1,0:T(8,128)(2,1)} %reshape.68), calls=%async_computation.3 | async-start | bytes 1572864 | tf_op jit(solution)/shard_map/all_to_all | solution.py:57
  126.0 0.2 select_reduce_fusion
  126.2 17.3 %all-to-all-done.3 = bf16[8,60,768]{2,1,0:T(8,128)(2,1)S(1)} async-done(((bf16[8,60,768]{2,1,0:T(8,128)(2,1)}), bf16[8,60,768]{2,1,0:T(8,128)(2,1)S(1)}, u32[]{:S(2)}, u32[]{:S(2)}) %all-to-all-start.3) | async-done | bytes 737312 | tf_op jit(solution)/shard_map/all_to_all | solution.py:57
  143.5 0.1 reshape.71
  143.6 0.8 fusion.11
  144.5 34.0 %all_to_all.33 = f32[16,12,768]{2,1,0:T(8,128)S(1)} all-to-all(f32[16,12,768]{2,1,0:T(8,128)S(1)} %fusion.11), channel_id=1, replica_groups=mesh['pipe'=16,'expert'=8,'dp'=8] {'pipe'}, dimensions={0} | all-to-all | bytes 1179648 | tf_op jit(solution)/shard_map/all_to_all | solution.py:72
  178.6 24.0 %all_to_all.34 = bf16[16,12,768]{2,1,0:T(8,128)(2,1)S(1)} all-to-all(bf16[16,12,768]{2,1,0:T(8,128)(2,1)S(1)} %broadcast_in_dim.5), channel_id=1, replica_groups=mesh['pipe'=16,'expert'=8,'dp'=8] {'pipe'}, dimensions={0} | all-to-all | bytes 589824 | tf_op jit(solution)/shard_map/all_to_all | solution.py:15
  202.5 0.8 reshape.70
  (15 shorter events, 0.4 us)
Async XLA Ops:
  0.0 118.5 %copy-start = (bf16[1,512,768]{2,1,0:T(8,128)(2,1)S(1)}, bf16[1,512,768]{2,1,0:T(8,128)(2,1)}, u32[]{:S(2)}) copy-start(bf16[1,512,768]{2,1,0:T(8,128)(2,1)} %param.11) | copy-start | bytes 2359300
  4.9 34.6 %copy-start.1 = (bf16[1,768,512]{2,1,0:T(8,128)(2,1)S(1)}, bf16[1,768,512]{2,1,0:T(8,128)(2,1)}, u32[]{:S(2)}) copy-start(bf16[1,768,512]{2,1,0:T(8,128)(2,1)} %param.10) | copy-start | bytes 2359300
  39.5 1.1 copy-start.2
  119.1 6.9 %copy-start.3 = (f32[192,2]{0,1:T(2,128)S(1)}, f32[192,2]{0,1:T(2,128)}, u32[]{:S(2)}) copy-start(f32[192,2]{0,1:T(2,128)} %param.8) | copy-start | bytes 4612
  120.1 23.4 %all-to-all-start.3 = ((bf16[8,60,768]{2,1,0:T(8,128)(2,1)}), bf16[8,60,768]{2,1,0:T(8,128)(2,1)S(1)}, u32[]{:S(2)}, u32[]{:S(2)}) async-start(bf16[8,60,768]{2,1,0:T(8,128)(2,1)} %reshape.68), calls=%async_computation.3 | async-start | bytes 1572864 | tf_op jit(solution)/shard_map/all_to_all | solution.py:57

commit v3 on v2

--- a/solution.py
+++ b/solution.py
@@ -45,13 +45,8 @@
     gate_part = jnp.dot(received, gate_proj[0], preferred_element_type=jnp.float32)
     up_part = jnp.dot(received, up_proj[0], preferred_element_type=jnp.float32)
     gate_up = jnp.concatenate([gate_part, up_part], axis=1)
-    n_dp = lax.axis_size("dp")
-    summed = jnp.sum(
-        lax.all_to_all(
-            gate_up.reshape(n_dp, slots_all // n_dp, -1), "dp", split_axis=0, concat_axis=0, tiled=True
-        ),
-        axis=0,
-    )
+    summed = lax.psum_scatter(gate_up, "dp", scatter_dimension=0, tiled=True)
+    summed = lax.optimization_barrier(summed)
     hidden = gather_rows(swiglu(summed), "dp")
     expert_part = jnp.dot(hidden, down_proj[0], preferred_element_type=jnp.float32)
     returned = lax.all_to_all(

time: 204 us -> 182 us (0.89)
  blocking collectives: 168 us -> 140 us
  starting transfers between devices: 5.88 us -> 9.78 us
    all_to_all x1 -> x0, blocking collectives: 56.8 us -> none  [body(): lax.all_to_all(gate_up.reshape(n_dp, slots_all // n_dp, -1), 'dp', split_...]
    unnamed x0 -> x1, blocking collectives: none -> 29.5 us
    unnamed x0 -> x1, starting transfers between devices: none -> 3.63 us
  transfers between devices with their start and end apart: 1 -> 2, of which waited for: 1 -> 2; matrix products, arithmetic and copies ran while one was open for 0% -> 1% of each run, Pallas kernels for 0% -> 0%
where the time goes in v3:
time: 182 us; the launch traced here: 181 us
  blocking collectives  140 us (77%)
  waiting for transfers between devices  17.8 us (10%)
  starting transfers between devices  9.78 us (5%)
  local copies, waits for them, and re-layouts  6.16 us (3%)
  matrix products  3.81 us (2%)
  other arithmetic  2.25 us (1%)
    all_to_all x2, blocking collectives, gather_rows(): lax.all_to_all(copies, axis, split_axis=0, concat_axis=0, tiled=True)  42.6 us
    all_to_all x1, blocking collectives, body(): lax.all_to_all(outbound, 'expert', split_axis=0, concat_axis=0, tiled=True)  34.4 us
    all_to_all x1, blocking collectives, body(): lax.all_to_all(combined.reshape(n_pipe, tok_rows // n_pipe, columns), 'pi...  34 us
    unnamed x1, blocking collectives  29.5 us
    all_to_all x1, waiting for transfers between devices, body(): lax.all_to_all(expert_part.astype(jnp.bfloat16).reshape(groups, capacity,...  17.3 us
    all_to_all x1, starting transfers between devices, body(): lax.all_to_all(expert_part.astype(jnp.bfloat16).reshape(groups, capacity,...  6.15 us
  transfers between devices with their start and end apart: 2, of which 2 were waited for; matrix products, arithmetic and copies ran while one was open for 1% of the time, Pallas kernels for 0%

profile of v3, /device:TPU:2, one launch (start us, length us, event | category | flops | bytes accessed | tf_op | source)
XLA Modules:
  0.0 181.1 jit_solution(7212407684073920136)
XLA Ops:
  0.0 0.9 copy.29
  0.9 0.1 eq.43
  1.0 0.1 eq.39
  1.2 0.9 reduce-window.6
  2.0 0.2 slice_reduce_fusion
  2.4 0.1 reduce_sum.42
  2.6 0.7 multiply_add_fusion
  3.3 0.1 fusion.7
  3.5 1.4 convolution_convert_fusion.1
  4.9 0.1 reshape.61
  5.0 34.4 %all_to_all.25 = bf16[8,60,768]{2,1,0:T(8,128)(2,1)S(1)} all-to-all(bf16[8,60,768]{2,1,0:T(8,128)(2,1)S(1)} %reshape.61), channel_id=1, replica_groups=mesh['pipe'=16,'expert'=8,'dp'=8] {'expert'}, dimensions={0} | all-to-all | bytes 1474560 | tf_op jit(solution)/shard_map/all_to_all | solution.py:42
  39.4 0.1 reshape.62
  39.5 0.5 fusion.2
  40.1 0.6 copy-done.2
  40.6 0.5 fusion.4
  41.2 0.1 pad_maximum_fusion
  41.3 29.5 %fusion = f32[64,1024]{1,0:T(8,128)S(1)} fusion(f32[480,1024]{1,0:T(8,128)S(1)} %pad_maximum_fusion), kind=kCustom, calls=%all-reduce-scatter | all-reduce-scatter fusion | flops 524289 | bytes 2232320
  70.8 3.6 %collective-permute-start = (f32[28,1024]{1,0:T(8,128)S(1)}, f32[28,1024]{1,0:T(8,128)S(1)}, u32[]{:S(2)}, u32[]{:S(2)}) collective-permute-start(f32[28,1024]{1,0:T(8,128)S(1)} %slice.19), channel_id=1, source_target_pairs={{0,1},{1,2},{2,3},{3,4},{4,5},{5,6},{6,7},{8,9},{9,10},{10,11},{11... | collective-permute-start | bytes 344072
  74.4 1.3 dynamic-slice.4
  76.4 0.6 collective-permute-done
  76.9 0.3 concatenate.4
  77.4 18.6 %all_to_all.26 = bf16[8,60,512]{2,1,0:T(8,128)(2,1)S(1)} all-to-all(bf16[8,60,512]{2,1,0:T(8,128)(2,1)S(1)} %broadcast_in_dim.4), channel_id=1, replica_groups=mesh['pipe'=16,'expert'=8,'dp'=8] {'dp'}, dimensions={0} | all-to-all | bytes 983040 | tf_op jit(solution)/shard_map/all_to_all | solution.py:15
  96.0 0.5 convolution_convert_fusion
  96.6 1.0 reshape.64
  97.6 6.2 %all-to-all-start.2 = ((bf16[8,60,768]{2,1,0:T(8,128)(2,1)}), bf16[8,60,768]{2,1,0:T(8,128)(2,1)S(1)}, u32[]{:S(2)}, u32[]{:S(2)}) async-start(bf16[8,60,768]{2,1,0:T(8,128)(2,1)} %reshape.64), calls=%async_computation.2 | async-start | bytes 1572864 | tf_op jit(solution)/shard_map/all_to_all | solution.py:52
  103.8 0.2 select_reduce_fusion
  104.0 17.3 %all-to-all-done.2 = bf16[8,60,768]{2,1,0:T(8,128)(2,1)S(1)} async-done(((bf16[8,60,768]{2,1,0:T(8,128)(2,1)}), bf16[8,60,768]{2,1,0:T(8,128)(2,1)S(1)}, u32[]{:S(2)}, u32[]{:S(2)}) %all-to-all-start.2) | async-done | bytes 737312 | tf_op jit(solution)/shard_map/all_to_all | solution.py:52
  121.3 0.1 reshape.67
  121.4 0.8 fusion.12
  122.2 34.0 %all_to_all.27 = f32[16,12,768]{2,1,0:T(8,128)S(1)} all-to-all(f32[16,12,768]{2,1,0:T(8,128)S(1)} %fusion.12), channel_id=1, replica_groups=mesh['pipe'=16,'expert'=8,'dp'=8] {'pipe'}, dimensions={0} | all-to-all | bytes 1179648 | tf_op jit(solution)/shard_map/all_to_all | solution.py:67
  156.3 24.0 %all_to_all.28 = bf16[16,12,768]{2,1,0:T(8,128)(2,1)S(1)} all-to-all(bf16[16,12,768]{2,1,0:T(8,128)(2,1)S(1)} %broadcast_in_dim.5), channel_id=1, replica_groups=mesh['pipe'=16,'expert'=8,'dp'=8] {'pipe'}, dimensions={0} | all-to-all | bytes 589824 | tf_op jit(solution)/shard_map/all_to_all | solution.py:15
  180.3 0.8 reshape.66
  (19 shorter events, 0.6 us)
Async XLA Ops:
  0.0 96.0 %copy-start = (bf16[1,512,768]{2,1,0:T(8,128)(2,1)S(1)}, bf16[1,512,768]{2,1,0:T(8,128)(2,1)}, u32[]{:S(2)}) copy-start(bf16[1,512,768]{2,1,0:T(8,128)(2,1)} %param.11) | copy-start | bytes 2359300
  4.9 34.6 %copy-start.1 = (bf16[1,768,512]{2,1,0:T(8,128)(2,1)S(1)}, bf16[1,768,512]{2,1,0:T(8,128)(2,1)}, u32[]{:S(2)}) copy-start(bf16[1,768,512]{2,1,0:T(8,128)(2,1)} %param.10) | copy-start | bytes 2359300
  39.5 1.1 copy-start.2
  70.8 6.1 %collective-permute-start = (f32[28,1024]{1,0:T(8,128)S(1)}, f32[28,1024]{1,0:T(8,128)S(1)}, u32[]{:S(2)}, u32[]{:S(2)}) collective-permute-start(f32[28,1024]{1,0:T(8,128)S(1)} %slice.19), channel_id=1, source_target_pairs={{0,1},{1,2},{2,3},{3,4},{4,5},{5,6},{6,7},{8,9},{9,10},{10,11},{11... | collective-permute-start | bytes 344072
  96.6 7.2 %copy-start.3 = (f32[192,2]{0,1:T(2,128)S(1)}, f32[192,2]{0,1:T(2,128)}, u32[]{:S(2)}) copy-start(f32[192,2]{0,1:T(2,128)} %param.8) | copy-start | bytes 4612
  97.6 23.7 %all-to-all-start.2 = ((bf16[8,60,768]{2,1,0:T(8,128)(2,1)}), bf16[8,60,768]{2,1,0:T(8,128)(2,1)S(1)}, u32[]{:S(2)}, u32[]{:S(2)}) async-start(bf16[8,60,768]{2,1,0:T(8,128)(2,1)} %reshape.64), calls=%async_computation.2 | async-start | bytes 1572864 | tf_op jit(solution)/shard_map/all_to_all | solution.py:52

commit v4 on v3

--- a/solution.py
+++ b/solution.py
@@ -49,32 +49,28 @@
     summed = lax.optimization_barrier(summed)
     hidden = gather_rows(swiglu(summed), "dp")
     expert_part = jnp.dot(hidden, down_proj[0], preferred_element_type=jnp.float32)
-    returned = lax.all_to_all(
-        expert_part.astype(jnp.bfloat16).reshape(groups, capacity, columns),
-        "expert",
-        split_axis=0,
-        concat_axis=0,
-        tiled=True,
-    ).reshape(slots_all, columns)
+    width = columns // n_pipe
+    outgoing = expert_part.astype(jnp.bfloat16).reshape(groups, capacity, n_pipe, width)
+    outgoing = jnp.transpose(outgoing, (2, 0, 1, 3)).reshape(n_pipe * groups, capacity, width)
+    arrived = lax.all_to_all(outgoing, ("pipe", "expert"), split_axis=0, concat_axis=0, tiled=True)
+    returned = jnp.sum(
+        arrived.reshape(n_pipe, slots_all, width).astype(jnp.float32), axis=0
+    )
     combined = lax.dot_general(
         weighting,
-        returned.astype(jnp.float32),
+        returned,
         (((1,), (0,)), ((), ())),
         precision=lax.Precision.HIGHEST,
         preferred_element_type=jnp.float32,
     )
-    share = jnp.sum(
-        lax.all_to_all(
-            combined.reshape(n_pipe, tok_rows // n_pipe, columns),
-            "pipe",
-            split_axis=0,
-            concat_axis=0,
-            tiled=True,
-        ),
-        axis=0,
-    )
-    return gather_rows(share.astype(jnp.bfloat16), "pipe")
+    return gather_cols(combined.astype(jnp.bfloat16), "pipe")
 
+
+def gather_cols(part, axis):
+    count = lax.axis_size(axis)
+    copies = jnp.broadcast_to(part[None], (count,) + part.shape)
+    gathered = lax.all_to_all(copies, axis, split_axis=0, concat_axis=0, tiled=True)
+    return jnp.transpose(gathered, (1, 0, 2)).reshape(part.shape[0], count * part.shape[1])
 
 def solution(mesh):
     return jax.shard_map(

time: 182 us -> 177 us (0.973)
  blocking collectives: 140 us -> 105 us
  local copies, waits for them, and re-layouts: 6.16 us -> 21.7 us
  starting transfers between devices: 9.78 us -> 17.8 us
  waiting for transfers between devices: 17.8 us -> 25.3 us
    all_to_all x2 -> x1, blocking collectives: 42.6 us -> 18.6 us  [gather_rows(): lax.all_to_all(copies, axis, split_axis=0, concat_axis=0, tiled=True)]
    all_to_all x1, blocking collectives: 34 us -> 22.8 us  [gather_cols(): lax.all_to_all(copies, axis, split_axis=0, concat_axis=0, tiled=True)]
    all_to_all x1, starting transfers between devices: 6.15 us -> 14.2 us  [body(): lax.all_to_all(outgoing, ('pipe', 'expert'), split_axis=0, concat_axis=0,...]
    all_to_all x1, waiting for transfers between devices: 17.3 us -> 24.7 us  [body(): lax.all_to_all(outgoing, ('pipe', 'expert'), split_axis=0, concat_axis=0,...]
    unnamed x13 -> x15, local copies, waits for them, and re-layouts: 3.04 us -> 10.2 us
    convert_element_type x0 -> x3, local copies, waits for them, and re-layouts: none -> 5.28 us  [the longest x2 5 us: body(): arrived.reshape(n_pipe, slots_all, width).astype(jnp.float32)]
where the time goes in v4:
time: 177 us
  blocking collectives  105 us (59%)
  waiting for transfers between devices  25.3 us (14%)
  local copies, waits for them, and re-layouts  21.7 us (12%)
  starting transfers between devices  17.8 us (10%)
  matrix products  3.49 us (2%)
  other arithmetic  2.52 us (1%)
    all_to_all x1, blocking collectives, body(): lax.all_to_all(outbound, 'expert', split_axis=0, concat_axis=0, tiled=True)  34.4 us
    unnamed x1, blocking collectives  29.5 us
    all_to_all x1, waiting for transfers between devices, body(): lax.all_to_all(outgoing, ('pipe', 'expert'), split_axis=0, concat_axis=0,...  24.7 us
    all_to_all x1, blocking collectives, gather_cols(): lax.all_to_all(copies, axis, split_axis=0, concat_axis=0, tiled=True)  22.8 us
    all_to_all x1, blocking collectives, gather_rows(): lax.all_to_all(copies, axis, split_axis=0, concat_axis=0, tiled=True)  18.6 us
    all_to_all x1, starting transfers between devices, body(): lax.all_to_all(outgoing, ('pipe', 'expert'), split_axis=0, concat_axis=0,...  14.2 us
    unnamed x15, local copies, waits for them, and re-layouts  10.2 us
    convert_element_type x2, local copies, waits for them, and re-layouts, body(): arrived.reshape(n_pipe, slots_all, width).astype(jnp.float32)  5 us
  transfers between devices with their start and end apart: 2, of which 2 were waited for; matrix products, arithmetic and copies ran while one was open for 1% of the time, Pallas kernels for 0%

profile of v4, /device:TPU:2, one launch (start us, length us, event | category | flops | bytes accessed | tf_op | source)
XLA Modules:
  0.0 176.9 jit_solution(2766522154082260222)
XLA Ops:
  0.0 0.9 copy.54
  1.2 0.9 reduce-window.6
  2.0 0.2 slice_reduce_fusion
  2.4 0.1 reduce_sum.42
  2.6 0.7 multiply_add_fusion
  3.5 1.4 convolution_convert_fusion.1
  5.0 34.4 %all_to_all.20 = bf16[8,60,768]{2,1,0:T(8,128)(2,1)S(1)} all-to-all(bf16[8,60,768]{2,1,0:T(8,128)(2,1)S(1)} %reshape.60), channel_id=1, replica_groups=mesh['pipe'=16,'expert'=8,'dp'=8] {'expert'}, dimensions={0} | all-to-all | bytes 1474560 | tf_op jit(solution)/shard_map/all_to_all | solution.py:42
  39.5 0.5 fusion.2
  40.1 0.6 copy-done.2
  40.6 0.5 fusion.4
  41.3 29.5 %fusion = f32[64,1024]{1,0:T(8,128)S(1)} fusion(f32[480,1024]{1,0:T(8,128)S(1)} %pad_maximum_fusion), kind=kCustom, calls=%all-reduce-scatter | all-reduce-scatter fusion | flops 524289 | bytes 2232320
  70.8 3.6 %collective-permute-start = (f32[28,1024]{1,0:T(8,128)S(1)}, f32[28,1024]{1,0:T(8,128)S(1)}, u32[]{:S(2)}, u32[]{:S(2)}) collective-permute-start(f32[28,1024]{1,0:T(8,128)S(1)} %slice.19), channel_id=1, source_target_pairs={{0,1},{1,2},{2,3},{3,4},{4,5},{5,6},{6,7},{8,9},{9,10},{10,11},{11... | collective-permute-start | bytes 344072
  74.4 1.3 dynamic-slice.4
  76.4 0.6 collective-permute-done
  76.9 0.3 concatenate.4
  77.4 18.6 %all_to_all.21 = bf16[8,60,512]{2,1,0:T(8,128)(2,1)S(1)} all-to-all(bf16[8,60,512]{2,1,0:T(8,128)(2,1)S(1)} %broadcast_in_dim.4), channel_id=1, replica_groups=mesh['pipe'=16,'expert'=8,'dp'=8] {'dp'}, dimensions={0} | all-to-all | bytes 983040 | tf_op jit(solution)/shard_map/all_to_all | solution.py:15
  96.0 0.5 convolution_convert_fusion
  96.6 0.3 copy.57
  96.9 1.5 reshape.63
  98.3 1.5 copy.58
  99.8 4.6 %reshape.69 = bf16[128,2,1440]{2,1,0:T(2,128)(2,1)} reshape(bf16[128,48,60]{2,1,0:T(8,128)(2,1)} %bitcast.40) | data formatting | bytes 1474560
  104.4 14.2 %all-to-all-start.2 = ((bf16[128,2,1440]{2,1,0:T(2,128)(2,1)}), bf16[128,2,1440]{2,1,0:T(2,128)(2,1)S(1)}, u32[]{:S(2)}, u32[]{:S(2)}) async-start(bf16[128,2,1440]{2,1,0:T(2,128)(2,1)} %reshape.69), calls=%async_computation.2 | async-start | bytes 1572864 | tf_op jit(solution)/shard_map/all_to_all | solution.py:55
  118.6 0.2 select_reduce_fusion
  118.8 24.7 %all-to-all-done.2 = bf16[128,2,1440]{2,1,0:T(2,128)(2,1)S(1)} async-done(((bf16[128,2,1440]{2,1,0:T(2,128)(2,1)}), bf16[128,2,1440]{2,1,0:T(2,128)(2,1)S(1)}, u32[]{:S(2)}, u32[]{:S(2)}) %all-to-all-start.2) | async-done | bytes 737312 | tf_op jit(solution)/shard_map/all_to_all | solution.py:55
  143.5 2.6 %reshape.70 = bf16[128,48,60]{2,1,0:T(8,128)(2,1)S(1)} reshape(bf16[128,2,1440]{2,1,0:T(2,128)(2,1)S(1)} %all-to-all-done.2) | data formatting | bytes 1474560
  146.2 1.2 copy.59
  147.4 2.1 %copy.60 = f32[128,60,48]{1,0,2:T(8,128)} copy(bf16[128,60,48]{0,2,1:T(8,128)(2,1)S(1)} %copy.59) | data formatting | bytes 2211840 | tf_op jit(solution)/shard_map/convert_element_type | solution.py:57
  149.5 2.9 %reshape.66 = f32[16,480,48]{1,0,2:T(8,128)S(1)} reshape(f32[128,60,48]{1,0,2:T(8,128)} %copy.60) | data formatting | bytes 2949120 | tf_op jit(solution)/shard_map/convert_element_type | solution.py:57
  152.4 0.3 reduce_sum.45
  152.7 0.5 convolution_convert_fusion.2
  153.3 22.8 %all_to_all.22 = bf16[16,192,48]{1,2,0:T(8,128)(2,1)S(1)} all-to-all(bf16[16,192,48]{1,2,0:T(8,128)(2,1)S(1)} %broadcast_in_dim.5), channel_id=1, replica_groups=mesh['pipe'=16,'expert'=8,'dp'=8] {'pipe'}, dimensions={0} | all-to-all | bytes 589824 | tf_op jit(solution)/shard_map/all_to_all | solution.py:72
  176.1 0.9 copy.61
  (23 shorter events, 1.3 us)
Async XLA Ops:
  0.0 96.0 %copy-start = (bf16[1,512,768]{2,1,0:T(8,128)(2,1)S(1)}, bf16[1,512,768]{2,1,0:T(8,128)(2,1)}, u32[]{:S(2)}) copy-start(bf16[1,512,768]{2,1,0:T(8,128)(2,1)} %param.11) | copy-start | bytes 2359300
  4.9 34.6 %copy-start.1 = (bf16[1,768,512]{2,1,0:T(8,128)(2,1)S(1)}, bf16[1,768,512]{2,1,0:T(8,128)(2,1)}, u32[]{:S(2)}) copy-start(bf16[1,768,512]{2,1,0:T(8,128)(2,1)} %param.10) | copy-start | bytes 2359300
  39.5 1.1 copy-start.2
  70.8 6.1 %collective-permute-start = (f32[28,1024]{1,0:T(8,128)S(1)}, f32[28,1024]{1,0:T(8,128)S(1)}, u32[]{:S(2)}, u32[]{:S(2)}) collective-permute-start(f32[28,1024]{1,0:T(8,128)S(1)} %slice.19), channel_id=1, source_target_pairs={{0,1},{1,2},{2,3},{3,4},{4,5},{5,6},{6,7},{8,9},{9,10},{10,11},{11... | collective-permute-start | bytes 344072
  99.8 18.8 %copy-start.3 = (f32[192,2]{0,1:T(2,128)S(1)}, f32[192,2]{0,1:T(2,128)}, u32[]{:S(2)}) copy-start(f32[192,2]{0,1:T(2,128)} %param.8) | copy-start | bytes 4612
  104.4 39.1 %all-to-all-start.2 = ((bf16[128,2,1440]{2,1,0:T(2,128)(2,1)}), bf16[128,2,1440]{2,1,0:T(2,128)(2,1)S(1)}, u32[]{:S(2)}, u32[]{:S(2)}) async-start(bf16[128,2,1440]{2,1,0:T(2,128)(2,1)} %reshape.69), calls=%async_computation.2 | async-start | bytes 1572864 | tf_op jit(solution)/shard_map/all_to_all | solution.py:55

commit v5 on v4

--- a/solution.py
+++ b/solution.py
@@ -54,12 +54,12 @@
     outgoing = jnp.transpose(outgoing, (2, 0, 1, 3)).reshape(n_pipe * groups, capacity, width)
     arrived = lax.all_to_all(outgoing, ("pipe", "expert"), split_axis=0, concat_axis=0, tiled=True)
     returned = jnp.sum(
-        arrived.reshape(n_pipe, slots_all, width).astype(jnp.float32), axis=0
+        arrived.reshape(n_pipe, groups, capacity, width).astype(jnp.float32), axis=0
     )
     combined = lax.dot_general(
-        weighting,
+        weighting.reshape(tok_rows, groups, capacity),
         returned,
-        (((1,), (0,)), ((), ())),
+        (((1, 2), (0, 1)), ((), ())),
         precision=lax.Precision.HIGHEST,
         preferred_element_type=jnp.float32,
     )

time: 177 us -> 172 us (0.972)
  local copies, waits for them, and re-layouts: 21.7 us -> 17.2 us
    convert_element_type x2 -> x0, local copies, waits for them, and re-layouts: 5 us -> none  [body(): arrived.reshape(n_pipe, slots_all, width).astype(jnp.float32)]
    unnamed x15 -> x17, local copies, waits for them, and re-layouts: 10.2 us -> 10.9 us
where the time goes in v5:
time: 172 us; the launch traced here: 171 us
  blocking collectives  105 us (61%)
  waiting for transfers between devices  24.2 us (14%)
  starting transfers between devices  17.8 us (10%)
  local copies, waits for them, and re-layouts  17.2 us (10%)
  matrix products  3.43 us (2%)
  other arithmetic  2.52 us (1%)
    all_to_all x1, blocking collectives, body(): lax.all_to_all(outbound, 'expert', split_axis=0, concat_axis=0, tiled=True)  34.4 us
    unnamed x1, blocking collectives  29.5 us
    all_to_all x1, waiting for transfers between devices, body(): lax.all_to_all(outgoing, ('pipe', 'expert'), split_axis=0, concat_axis=0,...  23.7 us
    all_to_all x1, blocking collectives, gather_cols(): lax.all_to_all(copies, axis, split_axis=0, concat_axis=0, tiled=True)  22.8 us
    all_to_all x1, blocking collectives, gather_rows(): lax.all_to_all(copies, axis, split_axis=0, concat_axis=0, tiled=True)  18.6 us
    all_to_all x1, starting transfers between devices, body(): lax.all_to_all(outgoing, ('pipe', 'expert'), split_axis=0, concat_axis=0,...  14.2 us
    unnamed x17, local copies, waits for them, and re-layouts  10.9 us
    unnamed x1, starting transfers between devices  3.63 us
  transfers between devices with their start and end apart: 2, of which 2 were waited for; matrix products, arithmetic and copies ran while one was open for 1% of the time, Pallas kernels for 0%

profile of v5, /device:TPU:2, one launch (start us, length us, event | category | flops | bytes accessed | tf_op | source)
XLA Modules:
  0.0 171.3 jit_solution(3733173093255213599)
XLA Ops:
  0.0 0.9 copy.35
  1.2 0.9 reduce-window.6
  2.0 0.2 slice_reduce_fusion
  2.4 0.1 reduce_sum.42
  2.6 0.7 multiply_add_fusion
  3.5 1.4 convolution_convert_fusion.1
  5.0 34.4 %all_to_all.20 = bf16[8,60,768]{2,1,0:T(8,128)(2,1)S(1)} all-to-all(bf16[8,60,768]{2,1,0:T(8,128)(2,1)S(1)} %reshape.64), channel_id=1, replica_groups=mesh['pipe'=16,'expert'=8,'dp'=8] {'expert'}, dimensions={0} | all-to-all | bytes 1474560 | tf_op jit(solution)/shard_map/all_to_all | solution.py:42
  39.5 0.5 fusion.3
  40.1 0.6 copy-done.3
  40.6 0.5 fusion.5
  41.3 29.5 %fusion = f32[64,1024]{1,0:T(8,128)S(1)} fusion(f32[480,1024]{1,0:T(8,128)S(1)} %pad_maximum_fusion), kind=kCustom, calls=%all-reduce-scatter | all-reduce-scatter fusion | flops 524289 | bytes 2232320
  70.8 3.6 %collective-permute-start = (f32[28,1024]{1,0:T(8,128)S(1)}, f32[28,1024]{1,0:T(8,128)S(1)}, u32[]{:S(2)}, u32[]{:S(2)}) collective-permute-start(f32[28,1024]{1,0:T(8,128)S(1)} %slice.19), channel_id=1, source_target_pairs={{0,1},{1,2},{2,3},{3,4},{4,5},{5,6},{6,7},{8,9},{9,10},{10,11},{11... | collective-permute-start | bytes 344072
  74.4 1.3 dynamic-slice.4
  76.4 0.6 collective-permute-done
  76.9 0.3 concatenate.4
  77.4 18.6 %all_to_all.21 = bf16[8,60,512]{2,1,0:T(8,128)(2,1)S(1)} all-to-all(bf16[8,60,512]{2,1,0:T(8,128)(2,1)S(1)} %broadcast_in_dim.4), channel_id=1, replica_groups=mesh['pipe'=16,'expert'=8,'dp'=8] {'dp'}, dimensions={0} | all-to-all | bytes 983040 | tf_op jit(solution)/shard_map/all_to_all | solution.py:15
  96.0 0.5 convolution_convert_fusion
  96.6 0.3 copy.39
  96.9 1.5 reshape.67
  98.3 1.5 copy.40
  99.8 4.6 %reshape.74 = bf16[128,2,1440]{2,1,0:T(2,128)(2,1)} reshape(bf16[128,48,60]{2,1,0:T(8,128)(2,1)} %bitcast.46) | data formatting | bytes 1474560
  104.4 14.2 %all-to-all-start.2 = ((bf16[128,2,1440]{2,1,0:T(2,128)(2,1)}), bf16[128,2,1440]{2,1,0:T(2,128)(2,1)S(1)}, u32[]{:S(2)}, u32[]{:S(2)}) async-start(bf16[128,2,1440]{2,1,0:T(2,128)(2,1)} %reshape.74), calls=%async_computation.2 | async-start | bytes 1572864 | tf_op jit(solution)/shard_map/all_to_all | solution.py:55
  118.6 0.2 select_reduce_fusion
  118.8 0.2 copy.38
  119.0 0.8 reshape.63
  119.9 23.7 %all-to-all-done.2 = bf16[128,2,1440]{2,1,0:T(2,128)(2,1)S(1)} async-done(((bf16[128,2,1440]{2,1,0:T(2,128)(2,1)}), bf16[128,2,1440]{2,1,0:T(2,128)(2,1)S(1)}, u32[]{:S(2)}, u32[]{:S(2)}) %all-to-all-start.2) | async-done | bytes 737312 | tf_op jit(solution)/shard_map/all_to_all | solution.py:55
  143.5 2.6 %reshape.75 = bf16[128,48,60]{2,1,0:T(8,128)(2,1)S(1)} reshape(bf16[128,2,1440]{2,1,0:T(2,128)(2,1)S(1)} %all-to-all-done.2) | data formatting | bytes 1474560
  146.2 0.3 convert_reduce_fusion
  146.5 0.7 copy-done.1
  147.2 0.4 fusion.1
  147.7 22.8 %all_to_all.22 = bf16[16,192,48]{1,2,0:T(8,128)(2,1)S(1)} all-to-all(bf16[16,192,48]{1,2,0:T(8,128)(2,1)S(1)} %broadcast_in_dim.5), channel_id=1, replica_groups=mesh['pipe'=16,'expert'=8,'dp'=8] {'pipe'}, dimensions={0} | all-to-all | bytes 589824 | tf_op jit(solution)/shard_map/all_to_all | solution.py:72
  170.5 0.9 copy.41
  (24 shorter events, 1.3 us)
Async XLA Ops:
  0.0 96.0 %copy-start = (bf16[1,512,768]{2,1,0:T(8,128)(2,1)S(1)}, bf16[1,512,768]{2,1,0:T(8,128)(2,1)}, u32[]{:S(2)}) copy-start(bf16[1,512,768]{2,1,0:T(8,128)(2,1)} %param.11) | copy-start | bytes 2359300
  4.9 34.6 %copy-start.2 = (bf16[1,768,512]{2,1,0:T(8,128)(2,1)S(1)}, bf16[1,768,512]{2,1,0:T(8,128)(2,1)}, u32[]{:S(2)}) copy-start(bf16[1,768,512]{2,1,0:T(8,128)(2,1)} %param.10) | copy-start | bytes 2359300
  39.5 1.1 copy-start.3
  70.8 6.1 %collective-permute-start = (f32[28,1024]{1,0:T(8,128)S(1)}, f32[28,1024]{1,0:T(8,128)S(1)}, u32[]{:S(2)}, u32[]{:S(2)}) collective-permute-start(f32[28,1024]{1,0:T(8,128)S(1)} %slice.19), channel_id=1, source_target_pairs={{0,1},{1,2},{2,3},{3,4},{4,5},{5,6},{6,7},{8,9},{9,10},{10,11},{11... | collective-permute-start | bytes 344072
  99.8 18.8 %copy-start.4 = (f32[192,2]{0,1:T(2,128)S(1)}, f32[192,2]{0,1:T(2,128)}, u32[]{:S(2)}) copy-start(f32[192,2]{0,1:T(2,128)} %param.8) | copy-start | bytes 4612
  104.4 39.1 %all-to-all-start.2 = ((bf16[128,2,1440]{2,1,0:T(2,128)(2,1)}), bf16[128,2,1440]{2,1,0:T(2,128)(2,1)S(1)}, u32[]{:S(2)}, u32[]{:S(2)}) async-start(bf16[128,2,1440]{2,1,0:T(2,128)(2,1)} %reshape.74), calls=%async_computation.2 | async-start | bytes 1572864 | tf_op jit(solution)/shard_map/all_to_all | solution.py:55
  146.2 1.0 copy-start.1

commit v6 on v5

--- a/solution.py
+++ b/solution.py
@@ -48,10 +48,14 @@
     summed = lax.psum_scatter(gate_up, "dp", scatter_dimension=0, tiled=True)
     summed = lax.optimization_barrier(summed)
     hidden = gather_rows(swiglu(summed), "dp")
-    expert_part = jnp.dot(hidden, down_proj[0], preferred_element_type=jnp.float32)
     width = columns // n_pipe
-    outgoing = expert_part.astype(jnp.bfloat16).reshape(groups, capacity, n_pipe, width)
-    outgoing = jnp.transpose(outgoing, (2, 0, 1, 3)).reshape(n_pipe * groups, capacity, width)
+    expert_part = jnp.einsum(
+        "srf,fpc->psrc",
+        hidden.reshape(groups, capacity, -1),
+        down_proj[0].reshape(-1, n_pipe, width),
+        preferred_element_type=jnp.float32,
+    )
+    outgoing = expert_part.astype(jnp.bfloat16).reshape(n_pipe * groups, capacity, width)
     arrived = lax.all_to_all(outgoing, ("pipe", "expert"), split_axis=0, concat_axis=0, tiled=True)
     returned = jnp.sum(
         arrived.reshape(n_pipe, groups, capacity, width).astype(jnp.float32), axis=0

time: 172 us -> 169 us (0.983)
  blocking collectives: 105 us -> 86.5 us
  waiting for transfers between devices: 24.2 us -> 39.3 us
  starting transfers between devices: 17.8 us -> 21.7 us
  local copies, waits for them, and re-layouts: 17.2 us -> 13.5 us
    all_to_all x1 -> x0, blocking collectives: 18.6 us -> none  [gather_rows(): lax.all_to_all(copies, axis, split_axis=0, concat_axis=0, tiled=True)]
    all_to_all x0 -> x1, waiting for transfers between devices: none -> 15.1 us  [gather_rows(): lax.all_to_all(copies, axis, split_axis=0, concat_axis=0, tiled=True)]
    all_to_all x0 -> x1, starting transfers between devices: none -> 3.73 us  [gather_rows(): lax.all_to_all(copies, axis, split_axis=0, concat_axis=0, tiled=True)]
    unnamed x17 -> x18, local copies, waits for them, and re-layouts: 10.9 us -> 9.58 us
  transfers between devices with their start and end apart: 2 -> 3, of which waited for: 2 -> 3; matrix products, arithmetic and copies ran while one was open for 1% -> 2% of each run, Pallas kernels for 0% -> 0%
where the time goes in v6:
time: 169 us; the launch traced here: 168 us
  blocking collectives  86.5 us (51%)
  waiting for transfers between devices  39.3 us (23%)
  starting transfers between devices  21.7 us (13%)
  local copies, waits for them, and re-layouts  13.5 us (8%)
  matrix products  3.88 us (2%)
  other arithmetic  2.52 us (1%)
    all_to_all x1, blocking collectives, body(): lax.all_to_all(outbound, 'expert', split_axis=0, concat_axis=0, tiled=True)  34.2 us
    unnamed x1, blocking collectives  29.5 us
    all_to_all x1, waiting for transfers between devices, body(): lax.all_to_all(outgoing, ('pipe', 'expert'), split_axis=0, concat_axis=0,...  23.7 us
    all_to_all x1, blocking collectives, gather_cols(): lax.all_to_all(copies, axis, split_axis=0, concat_axis=0, tiled=True)  22.8 us
    all_to_all x1, waiting for transfers between devices, gather_rows(): lax.all_to_all(copies, axis, split_axis=0, concat_axis=0, tiled=True)  15.1 us
    all_to_all x1, starting transfers between devices, body(): lax.all_to_all(outgoing, ('pipe', 'expert'), split_axis=0, concat_axis=0,...  14.2 us
    unnamed x18, local copies, waits for them, and re-layouts  9.58 us
    unnamed x1, starting transfers between devices  3.76 us
  transfers between devices with their start and end apart: 3, of which 3 were waited for; matrix products, arithmetic and copies ran while one was open for 2% of the time, Pallas kernels for 0%

profile of v6, /device:TPU:2, one launch (start us, length us, event | category | flops | bytes accessed | tf_op | source)
XLA Modules:
  0.0 168.2 jit_solution(8161317244641870593)
XLA Ops:
  0.0 0.9 copy.36
  1.2 0.9 reduce-window.6
  2.0 0.2 slice_reduce_fusion
  2.6 0.7 multiply_add_fusion
  3.5 1.4 convolution_convert_fusion.1
  5.0 34.2 %all_to_all.20 = bf16[8,60,768]{2,1,0:T(8,128)(2,1)S(1)} all-to-all(bf16[8,60,768]{2,1,0:T(8,128)(2,1)S(1)} %reshape.58), channel_id=1, replica_groups=mesh['pipe'=16,'expert'=8,'dp'=8] {'expert'}, dimensions={0} | all-to-all | bytes 1474560 | tf_op jit(solution)/shard_map/all_to_all | solution.py:42
  39.4 0.5 fusion.3
  39.9 0.4 copy-done.2
  40.4 0.5 fusion.5
  41.0 29.5 %fusion = f32[64,1024]{1,0:T(8,128)S(1)} fusion(f32[480,1024]{1,0:T(8,128)S(1)} %pad_maximum_fusion), kind=kCustom, calls=%all-reduce-scatter | all-reduce-scatter fusion | flops 524289 | bytes 2232320
  70.5 3.8 %collective-permute-start = (f32[28,1024]{1,0:T(8,128)S(1)}, f32[28,1024]{1,0:T(8,128)S(1)}, u32[]{:S(2)}, u32[]{:S(2)}) collective-permute-start(f32[28,1024]{1,0:T(8,128)S(1)} %slice.19), channel_id=1, source_target_pairs={{0,1},{1,2},{2,3},{3,4},{4,5},{5,6},{6,7},{8,9},{9,10},{10,11},{11... | collective-permute-start | bytes 344072
  74.3 1.3 dynamic-slice.4
  76.2 0.6 collective-permute-done
  76.8 0.3 concatenate.4
  77.2 0.8 broadcast_in_dim.4
  78.0 3.7 %all-to-all-start.1 = ((bf16[8,60,512]{2,1,0:T(8,128)(2,1)}), bf16[8,60,512]{2,1,0:T(8,128)(2,1)S(1)}, u32[]{:S(2)}, u32[]{:S(2)}) async-start(bf16[8,60,512]{2,1,0:T(8,128)(2,1)} %broadcast_in_dim.4), calls=%async_computation.1 | async-start | bytes 1048576 | tf_op jit(solution)/shard_map/all_to_all | solution.py:15
  81.7 0.3 copy.40
  82.0 15.1 %all-to-all-done.1 = bf16[8,60,512]{2,1,0:T(8,128)(2,1)S(1)} async-done(((bf16[8,60,512]{2,1,0:T(8,128)(2,1)}), bf16[8,60,512]{2,1,0:T(8,128)(2,1)S(1)}, u32[]{:S(2)}, u32[]{:S(2)}) %all-to-all-start.1) | async-done | bytes 491552 | tf_op jit(solution)/shard_map/all_to_all | solution.py:15
  97.1 1.0 fusion.1
  98.1 0.2 copy.41
  98.2 3.1 %reshape.68 = bf16[128,2,1440]{2,1,0:T(2,128)(2,1)} reshape(bf16[128,48,60]{2,1,0:T(8,128)(2,1)S(1)} %bitcast.49) | data formatting | bytes 1474560
  101.3 14.2 %all-to-all-start.2 = ((bf16[128,2,1440]{2,1,0:T(2,128)(2,1)}), bf16[128,2,1440]{2,1,0:T(2,128)(2,1)S(1)}, u32[]{:S(2)}, u32[]{:S(2)}) async-start(bf16[128,2,1440]{2,1,0:T(2,128)(2,1)} %reshape.68), calls=%async_computation.2 | async-start | bytes 1572864 | tf_op jit(solution)/shard_map/all_to_all | solution.py:59
  115.5 0.2 select_reduce_fusion
  115.7 0.2 copy.39
  115.9 0.8 reshape.57
  116.8 23.7 %all-to-all-done.2 = bf16[128,2,1440]{2,1,0:T(2,128)(2,1)S(1)} async-done(((bf16[128,2,1440]{2,1,0:T(2,128)(2,1)}), bf16[128,2,1440]{2,1,0:T(2,128)(2,1)S(1)}, u32[]{:S(2)}, u32[]{:S(2)}) %all-to-all-start.2) | async-done | bytes 737312 | tf_op jit(solution)/shard_map/all_to_all | solution.py:59
  140.4 2.6 %reshape.69 = bf16[128,48,60]{2,1,0:T(8,128)(2,1)S(1)} reshape(bf16[128,2,1440]{2,1,0:T(2,128)(2,1)S(1)} %all-to-all-done.2) | data formatting | bytes 1474560
  143.1 0.3 convert_reduce_fusion
  143.4 0.7 copy-done.1
  144.1 0.4 fusion.2
  144.6 22.8 %all_to_all.21 = bf16[16,192,48]{1,2,0:T(8,128)(2,1)S(1)} all-to-all(bf16[16,192,48]{1,2,0:T(8,128)(2,1)S(1)} %broadcast_in_dim.5), channel_id=1, replica_groups=mesh['pipe'=16,'expert'=8,'dp'=8] {'pipe'}, dimensions={0} | all-to-all | bytes 589824 | tf_op jit(solution)/shard_map/all_to_all | solution.py:76
  167.4 0.9 copy.42
  (23 shorter events, 1.3 us)
Async XLA Ops:
  0.0 39.4 %copy-start = (bf16[1,768,512]{2,1,0:T(8,128)(2,1)S(1)}, bf16[1,768,512]{2,1,0:T(8,128)(2,1)}, u32[]{:S(2)}) copy-start(bf16[1,768,512]{2,1,0:T(8,128)(2,1)} %param.10) | copy-start | bytes 2359300
  39.2 1.1 copy-start.2
  70.5 11.2 %copy-start.3 = (bf16[1,512,768]{2,1,0:T(8,128)(2,1)S(1)}, bf16[1,512,768]{2,1,0:T(8,128)(2,1)}, u32[]{:S(2)}) copy-start(bf16[1,512,768]{2,1,0:T(8,128)(2,1)} %param.11) | copy-start | bytes 2359300
  70.5 6.3 %collective-permute-start = (f32[28,1024]{1,0:T(8,128)S(1)}, f32[28,1024]{1,0:T(8,128)S(1)}, u32[]{:S(2)}, u32[]{:S(2)}) collective-permute-start(f32[28,1024]{1,0:T(8,128)S(1)} %slice.19), channel_id=1, source_target_pairs={{0,1},{1,2},{2,3},{3,4},{4,5},{5,6},{6,7},{8,9},{9,10},{10,11},{11... | collective-permute-start | bytes 344072
  78.0 19.1 %all-to-all-start.1 = ((bf16[8,60,512]{2,1,0:T(8,128)(2,1)}), bf16[8,60,512]{2,1,0:T(8,128)(2,1)S(1)}, u32[]{:S(2)}, u32[]{:S(2)}) async-start(bf16[8,60,512]{2,1,0:T(8,128)(2,1)} %broadcast_in_dim.4), calls=%async_computation.1 | async-start | bytes 1048576 | tf_op jit(solution)/shard_map/all_to_all | solution.py:15
  98.2 17.3 %copy-start.4 = (f32[192,2]{0,1:T(2,128)S(1)}, f32[192,2]{0,1:T(2,128)}, u32[]{:S(2)}) copy-start(f32[192,2]{0,1:T(2,128)} %param.8) | copy-start | bytes 4612
  101.3 39.1 %all-to-all-start.2 = ((bf16[128,2,1440]{2,1,0:T(2,128)(2,1)}), bf16[128,2,1440]{2,1,0:T(2,128)(2,1)S(1)}, u32[]{:S(2)}, u32[]{:S(2)}) async-start(bf16[128,2,1440]{2,1,0:T(2,128)(2,1)} %reshape.68), calls=%async_computation.2 | async-start | bytes 1572864 | tf_op jit(solution)/shard_map/all_to_all | solution.py:59
  143.1 1.0 copy-start.1

commit v7 on v6

--- a/solution.py
+++ b/solution.py
@@ -25,10 +25,12 @@
     slots_all = groups * capacity
     choices_flat = expert_ids.reshape(-1)
     onehot = (choices_flat[:, None] == jnp.arange(groups, dtype=jnp.int32)[None, :]).astype(
-        jnp.int32
+        jnp.bfloat16
     )
-    before = jnp.cumsum(onehot, axis=0) - onehot
-    slot_rank = jnp.sum(before * onehot, axis=1)
+    order = jnp.arange(choices_flat.shape[0], dtype=jnp.int32)
+    earlier = (order[None, :] < order[:, None]).astype(jnp.bfloat16)
+    before = jnp.dot(earlier, onehot, preferred_element_type=jnp.float32)
+    slot_rank = jnp.sum(before * onehot.astype(jnp.float32), axis=1).astype(jnp.int32)
     target = choices_flat * capacity + slot_rank
     placed = (target[:, None] == jnp.arange(slots_all, dtype=jnp.int32)[None, :]).reshape(
         tok_rows, 2, slots_all

time: 169 us -> 168 us (level)
  no operation moved by 1% of the time
where the time goes in v7:
time: 168 us; the launch traced here: 167 us
  blocking collectives  86.5 us (51%)
  waiting for transfers between devices  39.3 us (23%)
  starting transfers between devices  21.7 us (13%)
  local copies, waits for them, and re-layouts  13.1 us (8%)
  matrix products  4.08 us (2%)
    all_to_all x1, blocking collectives, body(): lax.all_to_all(outbound, 'expert', split_axis=0, concat_axis=0, tiled=True)  34.2 us
    unnamed x1, blocking collectives  29.5 us
    all_to_all x1, waiting for transfers between devices, body(): lax.all_to_all(outgoing, ('pipe', 'expert'), split_axis=0, concat_axis=0,...  23.7 us
    all_to_all x1, blocking collectives, gather_cols(): lax.all_to_all(copies, axis, split_axis=0, concat_axis=0, tiled=True)  22.8 us
    all_to_all x1, waiting for transfers between devices, gather_rows(): lax.all_to_all(copies, axis, split_axis=0, concat_axis=0, tiled=True)  15.1 us
    all_to_all x1, starting transfers between devices, body(): lax.all_to_all(outgoing, ('pipe', 'expert'), split_axis=0, concat_axis=0,...  14.2 us
    unnamed x18, local copies, waits for them, and re-layouts  9.58 us
    unnamed x1, starting transfers between devices  3.76 us
  transfers between devices with their start and end apart: 3, of which 3 were waited for; matrix products, arithmetic and copies ran while one was open for 2% of the time, Pallas kernels for 0%

profile of v7, /device:TPU:2, one launch (start us, length us, event | category | flops | bytes accessed | tf_op | source)
XLA Modules:
  0.0 167.1 jit_solution(10157328652280281973)
XLA Ops:
  0.0 0.9 copy.33
  1.0 0.2 fusion.3
  1.5 0.7 multiply_add_fusion
  2.2 0.1 fusion.10
  2.3 1.4 convolution_convert_fusion.1
  3.8 34.2 %all_to_all.20 = bf16[8,60,768]{2,1,0:T(8,128)(2,1)S(1)} all-to-all(bf16[8,60,768]{2,1,0:T(8,128)(2,1)S(1)} %reshape.43), channel_id=1, replica_groups=mesh['pipe'=16,'expert'=8,'dp'=8] {'expert'}, dimensions={0} | all-to-all | bytes 1474560 | tf_op jit(solution)/shard_map/all_to_all | solution.py:44
  38.2 0.5 fusion.4
  38.8 0.4 copy-done.2
  39.2 0.5 fusion.6
  39.9 29.5 %fusion = f32[64,1024]{1,0:T(8,128)S(1)} fusion(f32[480,1024]{1,0:T(8,128)S(1)} %pad_maximum_fusion), kind=kCustom, calls=%all-reduce-scatter | all-reduce-scatter fusion | flops 524289 | bytes 2232320
  69.4 3.8 %collective-permute-start = (f32[28,1024]{1,0:T(8,128)S(1)}, f32[28,1024]{1,0:T(8,128)S(1)}, u32[]{:S(2)}, u32[]{:S(2)}) collective-permute-start(f32[28,1024]{1,0:T(8,128)S(1)} %slice.10), channel_id=1, source_target_pairs={{0,1},{1,2},{2,3},{3,4},{4,5},{5,6},{6,7},{8,9},{9,10},{10,11},{11... | collective-permute-start | bytes 344072
  73.1 1.3 dynamic-slice.4
  75.1 0.6 collective-permute-done
  75.6 0.3 concatenate.4
  76.0 0.8 broadcast_in_dim.4
  76.8 3.7 %all-to-all-start.1 = ((bf16[8,60,512]{2,1,0:T(8,128)(2,1)}), bf16[8,60,512]{2,1,0:T(8,128)(2,1)S(1)}, u32[]{:S(2)}, u32[]{:S(2)}) async-start(bf16[8,60,512]{2,1,0:T(8,128)(2,1)} %broadcast_in_dim.4), calls=%async_computation.1 | async-start | bytes 1048576 | tf_op jit(solution)/shard_map/all_to_all | solution.py:15
  80.6 0.3 copy.36
  80.8 15.1 %all-to-all-done.1 = bf16[8,60,512]{2,1,0:T(8,128)(2,1)S(1)} async-done(((bf16[8,60,512]{2,1,0:T(8,128)(2,1)}), bf16[8,60,512]{2,1,0:T(8,128)(2,1)S(1)}, u32[]{:S(2)}, u32[]{:S(2)}) %all-to-all-start.1) | async-done | bytes 491552 | tf_op jit(solution)/shard_map/all_to_all | solution.py:15
  95.9 1.0 fusion.1
  96.9 0.2 copy.37
  97.1 3.1 %reshape.52 = bf16[128,2,1440]{2,1,0:T(2,128)(2,1)} reshape(bf16[128,48,60]{2,1,0:T(8,128)(2,1)S(1)} %bitcast.40) | data formatting | bytes 1474560
  100.2 14.2 %all-to-all-start.2 = ((bf16[128,2,1440]{2,1,0:T(2,128)(2,1)}), bf16[128,2,1440]{2,1,0:T(2,128)(2,1)S(1)}, u32[]{:S(2)}, u32[]{:S(2)}) async-start(bf16[128,2,1440]{2,1,0:T(2,128)(2,1)} %reshape.52), calls=%async_computation.2 | async-start | bytes 1572864 | tf_op jit(solution)/shard_map/all_to_all | solution.py:61
  114.4 0.2 select_reduce_fusion
  114.6 0.2 copy.35
  114.8 0.8 reshape.42
  115.6 23.7 %all-to-all-done.2 = bf16[128,2,1440]{2,1,0:T(2,128)(2,1)S(1)} async-done(((bf16[128,2,1440]{2,1,0:T(2,128)(2,1)}), bf16[128,2,1440]{2,1,0:T(2,128)(2,1)S(1)}, u32[]{:S(2)}, u32[]{:S(2)}) %all-to-all-start.2) | async-done | bytes 737312 | tf_op jit(solution)/shard_map/all_to_all | solution.py:61
  139.3 2.6 %reshape.53 = bf16[128,48,60]{2,1,0:T(8,128)(2,1)S(1)} reshape(bf16[128,2,1440]{2,1,0:T(2,128)(2,1)S(1)} %all-to-all-done.2) | data formatting | bytes 1474560
  141.9 0.3 convert_reduce_fusion
  142.2 0.7 copy-done.1
  143.0 0.4 fusion.2
  143.4 22.8 %all_to_all.21 = bf16[16,192,48]{1,2,0:T(8,128)(2,1)S(1)} all-to-all(bf16[16,192,48]{1,2,0:T(8,128)(2,1)S(1)} %broadcast_in_dim.5), channel_id=1, replica_groups=mesh['pipe'=16,'expert'=8,'dp'=8] {'pipe'}, dimensions={0} | all-to-all | bytes 589824 | tf_op jit(solution)/shard_map/all_to_all | solution.py:78
  166.2 0.9 copy.38
  (19 shorter events, 0.9 us)
Async XLA Ops:
  0.0 38.2 %copy-start = (bf16[1,768,512]{2,1,0:T(8,128)(2,1)S(1)}, bf16[1,768,512]{2,1,0:T(8,128)(2,1)}, u32[]{:S(2)}) copy-start(bf16[1,768,512]{2,1,0:T(8,128)(2,1)} %param.10) | copy-start | bytes 2359300
  38.1 1.1 copy-start.2
  69.3 11.2 %copy-start.3 = (bf16[1,512,768]{2,1,0:T(8,128)(2,1)S(1)}, bf16[1,512,768]{2,1,0:T(8,128)(2,1)}, u32[]{:S(2)}) copy-start(bf16[1,512,768]{2,1,0:T(8,128)(2,1)} %param.11) | copy-start | bytes 2359300
  69.4 6.3 %collective-permute-start = (f32[28,1024]{1,0:T(8,128)S(1)}, f32[28,1024]{1,0:T(8,128)S(1)}, u32[]{:S(2)}, u32[]{:S(2)}) collective-permute-start(f32[28,1024]{1,0:T(8,128)S(1)} %slice.10), channel_id=1, source_target_pairs={{0,1},{1,2},{2,3},{3,4},{4,5},{5,6},{6,7},{8,9},{9,10},{10,11},{11... | collective-permute-start | bytes 344072
  76.8 19.1 %all-to-all-start.1 = ((bf16[8,60,512]{2,1,0:T(8,128)(2,1)}), bf16[8,60,512]{2,1,0:T(8,128)(2,1)S(1)}, u32[]{:S(2)}, u32[]{:S(2)}) async-start(bf16[8,60,512]{2,1,0:T(8,128)(2,1)} %broadcast_in_dim.4), calls=%async_computation.1 | async-start | bytes 1048576 | tf_op jit(solution)/shard_map/all_to_all | solution.py:15
  97.1 17.3 %copy-start.4 = (f32[192,2]{0,1:T(2,128)S(1)}, f32[192,2]{0,1:T(2,128)}, u32[]{:S(2)}) copy-start(f32[192,2]{0,1:T(2,128)} %param.8) | copy-start | bytes 4612
  100.2 39.1 %all-to-all-start.2 = ((bf16[128,2,1440]{2,1,0:T(2,128)(2,1)}), bf16[128,2,1440]{2,1,0:T(2,128)(2,1)S(1)}, u32[]{:S(2)}, u32[]{:S(2)}) async-start(bf16[128,2,1440]{2,1,0:T(2,128)(2,1)} %reshape.52), calls=%async_computation.2 | async-start | bytes 1572864 | tf_op jit(solution)/shard_map/all_to_all | solution.py:61
  141.9 1.0 copy-start.1

commit v8 on v7

--- a/solution.py
+++ b/solution.py
@@ -23,18 +23,17 @@
     n_pipe = lax.axis_size("pipe")
     capacity = min(tok_rows, 5 * tok_rows // (2 * groups))
     slots_all = groups * capacity
-    choices_flat = expert_ids.reshape(-1)
-    onehot = (choices_flat[:, None] == jnp.arange(groups, dtype=jnp.int32)[None, :]).astype(
-        jnp.bfloat16
-    )
-    order = jnp.arange(choices_flat.shape[0], dtype=jnp.int32)
+    experts = jnp.arange(groups, dtype=jnp.int32)
+    first = (expert_ids[:, 0:1] == experts[None, :]).astype(jnp.bfloat16)
+    second = (expert_ids[:, 1:2] == experts[None, :]).astype(jnp.bfloat16)
+    order = jnp.arange(tok_rows, dtype=jnp.int32)
     earlier = (order[None, :] < order[:, None]).astype(jnp.bfloat16)
-    before = jnp.dot(earlier, onehot, preferred_element_type=jnp.float32)
-    slot_rank = jnp.sum(before * onehot.astype(jnp.float32), axis=1).astype(jnp.int32)
-    target = choices_flat * capacity + slot_rank
-    placed = (target[:, None] == jnp.arange(slots_all, dtype=jnp.int32)[None, :]).reshape(
-        tok_rows, 2, slots_all
-    )
+    before = jnp.dot(earlier, first + second, preferred_element_type=jnp.float32)
+    rank_first = jnp.sum(before * first.astype(jnp.float32), axis=1)
+    rank_second = jnp.sum((before + first.astype(jnp.float32)) * second.astype(jnp.float32), axis=1)
+    slot_rank = jnp.stack([rank_first, rank_second], axis=1).astype(jnp.int32)
+    target = expert_ids * capacity + slot_rank
+    placed = target[:, :, None] == jnp.arange(slots_all, dtype=jnp.int32)[None, None, :]
     dispatch_map = jnp.sum(placed.astype(jnp.bfloat16), axis=1)
     weighting = jnp.sum(placed.astype(jnp.float32) * gate_share[:, :, None], axis=1)
     outbound = lax.dot_general(

time: 168 us -> 167 us (level)
    unnamed x18 -> x17, local copies, waits for them, and re-layouts: 9.58 us -> 8.72 us
where the time goes in v8:
time: 167 us
  blocking collectives  86.5 us (52%)
  waiting for transfers between devices  39.3 us (24%)
  starting transfers between devices  21.7 us (13%)
  local copies, waits for them, and re-layouts  12.7 us (8%)
  matrix products  4.05 us (2%)
    all_to_all x1, blocking collectives, body(): lax.all_to_all(outbound, 'expert', split_axis=0, concat_axis=0, tiled=True)  34.2 us
    unnamed x1, blocking collectives  29.5 us
    all_to_all x1, waiting for transfers between devices, body(): lax.all_to_all(outgoing, ('pipe', 'expert'), split_axis=0, concat_axis=0,...  23.7 us
    all_to_all x1, blocking collectives, gather_cols(): lax.all_to_all(copies, axis, split_axis=0, concat_axis=0, tiled=True)  22.8 us
    all_to_all x1, waiting for transfers between devices, gather_rows(): lax.all_to_all(copies, axis, split_axis=0, concat_axis=0, tiled=True)  15.1 us
    all_to_all x1, starting transfers between devices, body(): lax.all_to_all(outgoing, ('pipe', 'expert'), split_axis=0, concat_axis=0,...  14.2 us
    unnamed x17, local copies, waits for them, and re-layouts  8.72 us
    unnamed x1, starting transfers between devices  3.76 us
  transfers between devices with their start and end apart: 3, of which 3 were waited for; matrix products, arithmetic and copies ran while one was open for 2% of the time, Pallas kernels for 0%

profile of v8, /device:TPU:2, one launch (start us, length us, event | category | flops | bytes accessed | tf_op | source)
XLA Modules:
  0.0 166.6 jit_solution(443238562915588380)
XLA Ops:
  0.0 0.8 fusion.22
  0.8 0.2 fusion.12
  1.0 0.7 fusion.21
  1.7 0.1 fusion.9
  1.8 1.4 convolution_convert_fusion.1
  3.3 34.2 %all_to_all.20 = bf16[8,60,768]{2,1,0:T(8,128)(2,1)S(1)} all-to-all(bf16[8,60,768]{2,1,0:T(8,128)(2,1)S(1)} %reshape.23), channel_id=1, replica_groups=mesh['pipe'=16,'expert'=8,'dp'=8] {'expert'}, dimensions={0} | all-to-all | bytes 1474560 | tf_op jit(solution)/shard_map/all_to_all | solution.py:43
  37.7 0.5 fusion.3
  38.3 0.4 copy-done.2
  38.7 0.5 fusion.5
  39.4 29.5 %fusion = f32[64,1024]{1,0:T(8,128)S(1)} fusion(f32[480,1024]{1,0:T(8,128)S(1)} %pad_maximum_fusion), kind=kCustom, calls=%all-reduce-scatter | all-reduce-scatter fusion | flops 524289 | bytes 2232320
  68.9 3.8 %collective-permute-start = (f32[28,1024]{1,0:T(8,128)S(1)}, f32[28,1024]{1,0:T(8,128)S(1)}, u32[]{:S(2)}, u32[]{:S(2)}) collective-permute-start(f32[28,1024]{1,0:T(8,128)S(1)} %slice.18), channel_id=1, source_target_pairs={{0,1},{1,2},{2,3},{3,4},{4,5},{5,6},{6,7},{8,9},{9,10},{10,11},{11... | collective-permute-start | bytes 344072
  72.6 1.3 dynamic-slice.4
  74.6 0.6 collective-permute-done
  75.1 0.3 concatenate.4
  75.5 0.8 broadcast_in_dim.4
  76.3 3.7 %all-to-all-start.1 = ((bf16[8,60,512]{2,1,0:T(8,128)(2,1)}), bf16[8,60,512]{2,1,0:T(8,128)(2,1)S(1)}, u32[]{:S(2)}, u32[]{:S(2)}) async-start(bf16[8,60,512]{2,1,0:T(8,128)(2,1)} %broadcast_in_dim.4), calls=%async_computation.1 | async-start | bytes 1048576 | tf_op jit(solution)/shard_map/all_to_all | solution.py:15
  80.1 0.3 copy.22
  80.3 15.1 %all-to-all-done.1 = bf16[8,60,512]{2,1,0:T(8,128)(2,1)S(1)} async-done(((bf16[8,60,512]{2,1,0:T(8,128)(2,1)}), bf16[8,60,512]{2,1,0:T(8,128)(2,1)S(1)}, u32[]{:S(2)}, u32[]{:S(2)}) %all-to-all-start.1) | async-done | bytes 491552 | tf_op jit(solution)/shard_map/all_to_all | solution.py:15
  95.4 1.0 fusion.1
  96.4 0.2 copy.23
  96.6 3.1 %reshape.32 = bf16[128,2,1440]{2,1,0:T(2,128)(2,1)} reshape(bf16[128,48,60]{2,1,0:T(8,128)(2,1)S(1)} %bitcast.44) | data formatting | bytes 1474560
  99.6 14.2 %all-to-all-start.2 = ((bf16[128,2,1440]{2,1,0:T(2,128)(2,1)}), bf16[128,2,1440]{2,1,0:T(2,128)(2,1)S(1)}, u32[]{:S(2)}, u32[]{:S(2)}) async-start(bf16[128,2,1440]{2,1,0:T(2,128)(2,1)} %reshape.32), calls=%async_computation.2 | async-start | bytes 1572864 | tf_op jit(solution)/shard_map/all_to_all | solution.py:60
  113.9 0.2 select_reduce_fusion
  114.1 0.2 copy.21
  114.3 0.8 reshape.22
  115.1 23.7 %all-to-all-done.2 = bf16[128,2,1440]{2,1,0:T(2,128)(2,1)S(1)} async-done(((bf16[128,2,1440]{2,1,0:T(2,128)(2,1)}), bf16[128,2,1440]{2,1,0:T(2,128)(2,1)S(1)}, u32[]{:S(2)}, u32[]{:S(2)}) %all-to-all-start.2) | async-done | bytes 737312 | tf_op jit(solution)/shard_map/all_to_all | solution.py:60
  138.8 2.6 %reshape.33 = bf16[128,48,60]{2,1,0:T(8,128)(2,1)S(1)} reshape(bf16[128,2,1440]{2,1,0:T(2,128)(2,1)S(1)} %all-to-all-done.2) | data formatting | bytes 1474560
  141.4 0.3 convert_reduce_fusion
  141.7 0.7 copy-done.1
  142.5 0.4 fusion.2
  142.9 22.8 %all_to_all.21 = bf16[16,192,48]{1,2,0:T(8,128)(2,1)S(1)} all-to-all(bf16[16,192,48]{1,2,0:T(8,128)(2,1)S(1)} %broadcast_in_dim.5), channel_id=1, replica_groups=mesh['pipe'=16,'expert'=8,'dp'=8] {'pipe'}, dimensions={0} | all-to-all | bytes 589824 | tf_op jit(solution)/shard_map/all_to_all | solution.py:77
  165.7 0.9 copy.24
  (15 shorter events, 0.5 us)
Async XLA Ops:
  0.0 37.7 %copy-start = (bf16[1,768,512]{2,1,0:T(8,128)(2,1)S(1)}, bf16[1,768,512]{2,1,0:T(8,128)(2,1)}, u32[]{:S(2)}) copy-start(bf16[1,768,512]{2,1,0:T(8,128)(2,1)} %param.10) | copy-start | bytes 2359300
  37.6 1.1 copy-start.2
  68.8 11.2 %copy-start.3 = (bf16[1,512,768]{2,1,0:T(8,128)(2,1)S(1)}, bf16[1,512,768]{2,1,0:T(8,128)(2,1)}, u32[]{:S(2)}) copy-start(bf16[1,512,768]{2,1,0:T(8,128)(2,1)} %param.11) | copy-start | bytes 2359300
  68.9 6.3 %collective-permute-start = (f32[28,1024]{1,0:T(8,128)S(1)}, f32[28,1024]{1,0:T(8,128)S(1)}, u32[]{:S(2)}, u32[]{:S(2)}) collective-permute-start(f32[28,1024]{1,0:T(8,128)S(1)} %slice.18), channel_id=1, source_target_pairs={{0,1},{1,2},{2,3},{3,4},{4,5},{5,6},{6,7},{8,9},{9,10},{10,11},{11... | collective-permute-start | bytes 344072
  76.3 19.1 %all-to-all-start.1 = ((bf16[8,60,512]{2,1,0:T(8,128)(2,1)}), bf16[8,60,512]{2,1,0:T(8,128)(2,1)S(1)}, u32[]{:S(2)}, u32[]{:S(2)}) async-start(bf16[8,60,512]{2,1,0:T(8,128)(2,1)} %broadcast_in_dim.4), calls=%async_computation.1 | async-start | bytes 1048576 | tf_op jit(solution)/shard_map/all_to_all | solution.py:15
  96.6 17.3 %copy-start.4 = (f32[192,2]{0,1:T(2,128)S(1)}, f32[192,2]{0,1:T(2,128)}, u32[]{:S(2)}) copy-start(f32[192,2]{0,1:T(2,128)} %param.8) | copy-start | bytes 4612
  99.6 39.1 %all-to-all-start.2 = ((bf16[128,2,1440]{2,1,0:T(2,128)(2,1)}), bf16[128,2,1440]{2,1,0:T(2,128)(2,1)S(1)}, u32[]{:S(2)}, u32[]{:S(2)}) async-start(bf16[128,2,1440]{2,1,0:T(2,128)(2,1)} %reshape.32), calls=%async_computation.2 | async-start | bytes 1572864 | tf_op jit(solution)/shard_map/all_to_all | solution.py:60
  141.4 1.0 copy-start.1
